TPU v7x, 32 devices: a whole 2x2x4 slice. The times are simulated.
32 devices in a mesh: groups: 2 (over y), expert: 4 (over z), dp: 4 (over x, core).
Axes of the slice: x: 2, y: 2, z: 4, core: 2. Of those that a mesh axis runs over, the one named last changes fastest.
Arguments:
- out_grad: bfloat16 [4096, 2048], P(('groups', 'expert', 'dp')), parts along dimension 0, may hold values from -0.5 to 0.5
- gate_weights: bfloat16 [4096, 8], P(('groups', 'expert', 'dp')), parts along dimension 0, may hold values from 0.049804688 to 0.5
- expert_ids: int32 [4096, 8], P(('groups', 'expert', 'dp')), parts along dimension 0, may hold values from 0 to 31, all different within a row; in each aligned block of 128 rows (0 to 127, 128 to 255, ...) at most 36 rows name the same one
- hidden: bfloat16 [32, 8, 4, 36, 768], P('expert', ('groups', 'dp')), parts along dimension 1, may hold values from -6 to 6
- down_weight: bfloat16 [32, 768, 2048], P('expert', None, 'dp'), may hold values from -0.21875 to 0.21875
Outputs:
- weight_grad: float32 [64, 768, 2048], P(('groups', 'expert'), None, 'dp'), parts along dimension 0
- gate_grad: float32 [4096, 8], P(('groups', 'expert', 'dp')), parts along dimension 0
There are 2 independent parts, one for each index of `groups`. A program takes and returns all parts, laid end to end along the dimension named above; an argument that names none is the same for every part. Nothing has to cross between parts.
Inputs may be any that keep to these rules, and one draw needn't show every extreme that they name: `expert_ids`: each token names 8 different experts; within each block of 128 tokens (one device's tokens) no expert is named by more than 36 tokens, a bound that some block reaches.
All inputs are finite; a program needn't handle non-finite values.
Results may differ from a plain program's by a relative error of at most 0.0095.
Values may be sent and summed in bfloat16 or wider, within the bound.
No kernel may reach another device: no remote copies, remote signals or barrier semaphores. Data moves between devices by JAX's collectives and lax.ppermute only.
A program may use at most 128 MiB of HBM per device.

v0:
```python
import jax
import jax.numpy as jnp
from jax import lax
from jax.sharding import PartitionSpec as P


def per_device(out_grad, gate_weights, expert_ids, hidden, down_weight):
    tok_rows, top_count = expert_ids.shape
    row_width = out_grad.shape[1]
    local_count = hidden.shape[0]
    source_count = hidden.shape[2]
    capacity = hidden.shape[3]
    hidden_width = hidden.shape[4]
    peer_count = lax.axis_size("expert")
    shards = lax.axis_size("dp")
    expert_count = local_count * peer_count
    col_width = row_width // shards
    block_count = peer_count * shards
    f32 = jnp.float32
    bf16 = jnp.bfloat16
    cols = out_grad.reshape(tok_rows, shards, col_width)
    cols = lax.all_to_all(cols, "dp", split_axis=1, concat_axis=0, tiled=True)
    cols = cols.reshape(shards, tok_rows, col_width)
    grad_all = lax.all_gather(cols, "expert", axis=0, tiled=False)
    grad_all = grad_all.reshape(block_count, tok_rows, col_width)
    ids_all = lax.all_gather(expert_ids, ("expert", "dp"), axis=0, tiled=True)
    ids_all = ids_all.reshape(block_count, tok_rows, top_count)
    gate_all = lax.all_gather(gate_weights, ("expert", "dp"), axis=0, tiled=True)
    gate_all = gate_all.reshape(block_count, tok_rows, top_count)
    hidden_all = lax.all_gather(hidden, "dp", axis=1, tiled=True)
    my_experts = lax.axis_index("expert") * local_count + jnp.arange(local_count, dtype=jnp.int32)
    hit = ids_all[:, :, :, None] == my_experts[None, None, None, :]
    chose = jnp.any(hit, axis=2)
    gate_hit = jnp.sum(jnp.where(hit, gate_all.astype(f32)[:, :, :, None], 0.0), axis=2)
    before = (jnp.arange(tok_rows)[:, None] < jnp.arange(tok_rows)[None, :]).astype(bf16)
    rank = jnp.einsum("bul,ut->btl", chose.astype(bf16), before, preferred_element_type=f32).astype(
        jnp.int32
    )
    slot_ids = jnp.arange(capacity, dtype=jnp.int32)
    chose_t = chose.transpose(0, 2, 1)
    rank_t = rank.transpose(0, 2, 1)
    gate_t = gate_hit.transpose(0, 2, 1)
    select = chose_t[:, :, None, :] & (rank_t[:, :, None, :] == slot_ids[None, None, :, None])
    select_gate = jnp.where(select, gate_t[:, :, None, :], 0.0).astype(bf16)
    grad_rows = jnp.einsum(
        "blct,btd->blcd", select.astype(bf16), grad_all, preferred_element_type=f32
    ).astype(bf16)
    scaled = jnp.einsum("blct,btd->blcd", select_gate, grad_all, preferred_element_type=f32).astype(
        bf16
    )
    grad_rows = grad_rows.reshape(peer_count, shards, local_count, capacity, col_width)
    scaled = scaled.reshape(peer_count, shards, local_count, capacity, col_width)
    weight_grad = None
    for replica in range(shards):
        part = (
            jnp.einsum(
                "lscf,slcd->lfd",
                hidden_all[:, replica],
                scaled[:, replica],
                preferred_element_type=f32,
            )
            .astype(bf16)
            .astype(f32)
        )
        weight_grad = part if weight_grad is None else weight_grad + part
    expert_out = jnp.einsum("liscf,lfd->silcd", hidden_all, down_weight, preferred_element_type=f32)
    slot_part = jnp.sum(grad_rows.astype(f32) * expert_out, axis=4)
    send_back = slot_part.reshape(block_count, local_count, capacity)
    returned = lax.all_to_all(send_back, ("expert", "dp"), split_axis=0, concat_axis=0, tiled=True)
    returned = returned.reshape(peer_count, shards, local_count, capacity)
    slot_grad = jnp.sum(returned, axis=1).reshape(expert_count * capacity)
    own_chose = jnp.any(
        expert_ids[:, :, None] == jnp.arange(expert_count, dtype=jnp.int32)[None, None, :], axis=1
    )
    own_rank = jnp.einsum(
        "ue,ut->te", own_chose.astype(bf16), before, preferred_element_type=f32
    ).astype(jnp.int32)
    own_slot = jnp.take_along_axis(own_rank, expert_ids, axis=1)
    gate_grad = slot_grad[expert_ids * capacity + own_slot]
    return (weight_grad, gate_grad)


def solution(mesh):
    return jax.shard_map(
        per_device,
        mesh=mesh,
        in_specs=(
            P(("groups", "expert", "dp"), None),
            P(("groups", "expert", "dp"), None),
            P(("groups", "expert", "dp"), None),
            P("expert", ("groups", "dp"), None, None, None),
            P("expert", None, "dp"),
        ),
        out_specs=(P(("groups", "expert"), None, "dp"), P(("groups", "expert", "dp"), None)),
        check_vma=False,
    )
```

profile of v0, /device:TPU:0, one launch (start us, length us, event | category | flops | bytes accessed | tf_op | source)
XLA Modules:
  0.0 189.4 jit_solution(14676324695385926704)
XLA Ops:
  7.2 0.0 copy-start.1
  7.2 0.0 all-gather.6.cloned.1.call-start
  7.2 1.4 copy.113
  8.7 12.9 %all_to_all.20 = bf16[128,4,512]{0,2,1:T(8,128)(2,1)S(1)} all-to-all(bf16[128,4,512]{0,2,1:T(8,128)(2,1)S(1)} %bitcast.95), channel_id=1, replica_groups=mesh['groups'=2,'expert'=4,'dp'=4] {'dp'}, dimensions={1} | all-to-all | bytes 1048576 | tf_op jit(solution)/shard_map/all_to_all | solution.py:22
  21.5 1.0 copy.114
  22.5 0.0 all-gather.6.cloned.1.call-update
  22.6 0.0 copy-start.4
  22.6 0.0 all-gather.4.cloned.1.call-start
  22.6 0.0 copy-done.1
  22.6 1.8 copy.116
  24.4 0.0 all-gather.4.cloned.1.call-update
  24.4 0.0 copy-done.4
  24.5 0.1 copy.127
  24.6 0.1 reshape.69
  24.7 0.1 convolution_convert_fusion.3
  24.8 0.0 copy-start.5
  24.8 7.0 %gather_fusion.1 = s32[1024]{0:T(1024)S(1)} fusion(s32[128,32]{0,1:T(8,128)S(1)} %convolution_convert_fusion.3, s32[1024]{0:T(1024)S(1)} %reshape.69), kind=kCustom, calls=%fused_computation.1 | custom fusion | bytes 16384 | tf_op jit(solution)/shard_map/jit(take_along_axis)/gather | solution.py:78
  31.9 0.1 reshape.72
  32.0 0.1 copy.129
  32.1 0.1 reshape.63
  32.2 0.0 copy-done.5
  32.2 21.2 %all_gather.13 = bf16[2048,8]{0,1:T(8,128)(2,1)S(1)} all-gather(bf16[128,8]{0,1:T(8,128)(2,1)S(1)} %copy-done.5), channel_id=1, replica_groups=mesh['groups'=2,'expert'=4,'dp'=4] {'expert','dp'}, dimensions={0}, use_global_device_ids=true | all-gather | bytes 34816 | tf_op jit(solution)/shard_map/all_gather | solution.py:28
  53.4 18.1 %all_gather.12 = s32[2048,8]{0,1:T(8,128)S(1)} all-gather(s32[128,8]{0,1:T(8,128)S(1)} %copy-done.4), channel_id=1, replica_groups=mesh['groups'=2,'expert'=4,'dp'=4] {'expert','dp'}, dimensions={0}, use_global_device_ids=true | all-gather | bytes 69632 | tf_op jit(solution)/shard_map/all_gather | solution.py:26
  71.5 0.1 compare_reduce_fusion
  71.7 0.1 fusion.21
  71.8 0.1 convolution_convert_fusion.2
  72.0 0.0 all-gather.6.cloned.1.call-done
  72.0 3.1 %convolution_convert_fusion = bf16[16,8,36,512]{3,2,1,0:T(8,128)(2,1)S(1)} fusion(bf16[16,128,1,512]{3,1,2,0:T(8,128)(2,1)} %all-gather.6.cloned.1.call-done, bf16[16,8,128]{2,1,0:T(8,128)(2,1)S(1)} %bitcast.101, s32[16,8,128]{2,1,0:T(8,128)S(1)} %convolution_convert_fusion.2, pred[16,8,128]{2,1,0:T(8,128)(4,1)S(1)} %bitcast.98), kind=kOutput, calls=%fused_computation.12 | convolution fusion | flops 608108544 | bytes 6930432 | tf_op jit(solution)/shard_map/blct,btd->blcd/dot_general | solution.py:48
  75.1 0.0 copy-start
  75.1 2.0 %fusion.27 = (bf16[4,1,8,36,512]{4,3,2,1,0:T(8,128)(2,1)S(1)}, bf16[4,1,8,36,512]{4,3,2,1,0:T(8,128)(2,1)}, bf16[4,1,8,36,512]{4,3,2,1,0:T(8,128)(2,1)}, bf16[4,1,8,36,512]{4,3,2,1,0:T(8,128)(2,1)S(1)}) fusion(bf16[4,4,8,36,512]{4,3,2,1,0:T(8,128)(2,1)S(1)} %bitcast.93), kind=kLoop, calls=%fused_computation.55 | loop fusion | bytes 9437184 | tf_op jit(solution)/shard_map/slice | solution.py:59
  77.1 0.5 copy-done
  77.6 6.0 %bitcast_convert_fusion.5 = f32[4,4,8,36,512]{4,3,2,1,0:T(8,128)} fusion(bf16[16,128,1,512]{3,1,2,0:T(8,128)(2,1)S(1)} %copy-done, s32[16,8,128]{2,1,0:T(8,128)S(1)} %convolution_convert_fusion.2, pred[16,8,128]{2,1,0:T(8,128)(4,1)S(1)} %bitcast.99), kind=kOutput, calls=%fused_computation.52 | convolution fusion | flops 609878016 | bytes 11616256 | tf_op jit(solution)/shard_map/blct,btd->blcd/dot_general | solution.py:45
  83.7 37.0 %all-gather.4.cloned.1.call-done = bf16[8,4,4,36,768]{4,0,3,2,1:T(8,128)(2,1)} async-done(((bf16[8,1,4,36,768]{4,0,3,2,1:T(8,128)(2,1)}), bf16[8,4,4,36,768]{4,0,3,2,1:T(8,128)(2,1)}) %all-gather.4.cloned.1.call-update) | async-done | bytes 7077904 | tf_op jit(solution)/shard_map/all_gather | solution.py:30
  120.7 11.1 %fusion = f32[4,4,8,36]{3,0,1,2:T(4,128)S(1)} fusion(f32[4,4,8,36,512]{4,3,2,1,0:T(8,128)} %bitcast_convert_fusion.5, bf16[8,4,4,36,768]{4,0,3,2,1:T(8,128)(2,1)} %all-gather.4.cloned.1.call-done, bf16[8,768,512]{2,1,0:T(8,128)(2,1)} %param.9), kind=kOutput, calls=%fused_computation.8 | convolution fusion | flops 3628592640 | bytes 22824960 | tf_op jit(solution)/shard_map/liscf,lfd->silcd/dot_general | solution.py:66
  131.8 0.7 reshape.91
  132.5 4.7 %all-to-all-start.1 = ((f32[16,1,288]{2,1,0:T(1,128)}), f32[16,1,288]{2,1,0:T(1,128)S(1)}, u32[]{:S(2)}, u32[]{:S(2)}) async-start(f32[16,1,288]{2,1,0:T(1,128)} %reshape.91), calls=%async_computation.1 | async-start | bytes 49152 | tf_op jit(solution)/shard_map/all_to_all | solution.py:69
  137.3 0.0 copy-start.3
  137.3 3.6 %fusion.26 = (bf16[8,1,4,36,768]{4,0,3,2,1:T(8,128)(2,1)S(1)}, bf16[8,1,4,36,768]{4,0,3,2,1:T(8,128)(2,1)S(1)}, bf16[8,1,4,36,768]{4,0,3,2,1:T(8,128)(2,1)S(1)}, bf16[8,1,4,36,768]{4,0,3,2,1:T(8,128)(2,1)S(1)}) fusion(bf16[8,4,4,36,768]{4,0,3,2,1:T(8,128)(2,1)} %all-gather.4.cloned.1.call-done), kind=kLoop, calls=%fused_computation.54 | loop fusion | bytes 14155776 | tf_op jit(solution)/shard_map/slice | solution.py:58
  140.9 0.0 copy-done.3
  140.9 0.0 copy-start.2
  140.9 2.0 %fusion.12 = bf16[8,512,768,1]{2,1,3,0:T(8,128)(2,1)S(1)} fusion(bf16[8,1,4,36,768]{4,0,3,2,1:T(8,128)(2,1)S(1)} %get-tuple-element.15, bf16[4,1,8,36,512]{4,3,2,1,0:T(8,128)(2,1)S(1)} %copy-done.3), kind=kOutput, calls=%fused_computation.21 | convolution fusion | flops 905969664 | bytes 9240576 | tf_op jit(solution)/shard_map/lscf,slcd->lfd/dot_general | solution.py:56
  143.0 0.0 copy-done.2
  143.0 4.7 %fusion.13 = bf16[8,512,768,1]{2,1,3,0:T(8,128)(2,1)} fusion(bf16[8,1,4,36,768]{4,0,3,2,1:T(8,128)(2,1)S(1)} %get-tuple-element.16, bf16[4,1,8,36,512]{4,3,2,1,0:T(8,128)(2,1)S(1)} %copy-done.2), kind=kOutput, calls=%fused_computation.23 | convolution fusion | flops 905969664 | bytes 9240576 | tf_op jit(solution)/shard_map/lscf,slcd->lfd/dot_general | solution.py:56
  147.6 4.8 %fusion.14 = bf16[8,512,768,1]{2,1,3,0:T(8,128)(2,1)} fusion(bf16[8,1,4,36,768]{4,0,3,2,1:T(8,128)(2,1)S(1)} %get-tuple-element.17, bf16[4,1,8,36,512]{4,3,2,1,0:T(8,128)(2,1)S(1)} %get-tuple-element.21), kind=kOutput, calls=%fused_computation.25 | convolution fusion | flops 905969664 | bytes 9240576 | tf_op jit(solution)/shard_map/lscf,slcd->lfd/dot_general | solution.py:56
  152.4 9.2 %add_bitcast_fusion = f32[8,768,512]{1,2,0:T(8,128)} fusion(bf16[8,512,768,1]{2,1,3,0:T(8,128)(2,1)} %fusion.14, bf16[8,512,768,1]{2,1,3,0:T(8,128)(2,1)} %fusion.13, bf16[8,512,768,1]{2,1,3,0:T(8,128)(2,1)S(1)} %fusion.12, bf16[8,1,4,36,768]{4,0,3,2,1:T(8,128)(2,1)S(1)} %get-tuple-element.14, bf16[4,1,8,36,512]{4,3,2,1,0:T(8,128)(2,1)S(1)} %get-tuple-element.18), kind=kOutput, calls=%fused_computation.6 | convolution fusion | flops 931135488 | bytes 34406400 | tf_op jit(solution)/shard_map/lscf,slcd->lfd/dot_general | solution.py:56
  161.6 12.6 %copy.130 = f32[8,768,512]{2,1,0:T(8,128)} copy(f32[8,768,512]{1,2,0:T(8,128)} %add_bitcast_fusion) | data formatting | bytes 25165824
  174.2 0.0 all-to-all-done.1
  174.2 0.5 broadcast.36
  174.7 0.7 reduce
  175.5 0.1 reshape.92
  175.6 0.1 reshape.57
  175.7 6.2 %gather_fusion = f32[1024]{0:T(1024)S(1)} fusion(f32[1152]{0:T(1024)S(1)} %reshape.57, s32[1024]{0:T(1024)S(1)} %broadcast_clamp_fusion), kind=kCustom, calls=%fused_computation | custom fusion | bytes 12288 | tf_op jit(solution)/shard_map/gather | solution.py:79
  181.8 0.1 reshape.62
  181.9 0.7 copy.131
  (9 shorter events, 0.1 us)
Async XLA Ops:
  7.2 15.5 %copy-start.1 = (bf16[8,1,4,36,768]{4,2,3,1,0:T(4,128)(2,1)S(1)}, bf16[8,1,4,36,768]{4,2,3,1,0:T(4,128)(2,1)}, u32[]{:S(2)}) copy-start(bf16[8,1,4,36,768]{4,2,3,1,0:T(4,128)(2,1)} %param.8) | copy-start | bytes 5308420
  7.2 64.8 %all-gather.6.cloned.1.call-start = ((), (), s32[]{:S(2)}) async-start(), calls=%async_computation.3 | async-start | bytes 2621440 | tf_op jit(solution)/shard_map/all_gather | solution.py:24
  22.6 1.9 copy-start.4
  22.6 98.1 %all-gather.4.cloned.1.call-start = ((), (), s32[]{:S(2)}) async-start(), calls=%async_computation.2 | async-start | bytes 8847360 | tf_op jit(solution)/shard_map/all_gather | solution.py:30
  24.8 7.4 %copy-start.5 = (bf16[128,8]{0,1:T(8,128)(2,1)S(1)}, bf16[128,8]{0,1:T(8,128)(2,1)}, u32[]{:S(2)}) copy-start(bf16[128,8]{0,1:T(8,128)(2,1)} %param.6) | copy-start | bytes 6148
  75.1 2.5 %copy-start = (bf16[16,128,1,512]{3,1,2,0:T(8,128)(2,1)S(1)}, bf16[16,128,1,512]{3,1,2,0:T(8,128)(2,1)}, u32[]{:S(2)}) copy-start(bf16[16,128,1,512]{3,1,2,0:T(8,128)(2,1)} %all-gather.6.cloned.1.call-done) | copy-start | bytes 6291460
  132.5 41.7 %all-to-all-start.1 = ((f32[16,1,288]{2,1,0:T(1,128)}), f32[16,1,288]{2,1,0:T(1,128)S(1)}, u32[]{:S(2)}, u32[]{:S(2)}) async-start(f32[16,1,288]{2,1,0:T(1,128)} %reshape.91), calls=%async_computation.1 | async-start | bytes 49152 | tf_op jit(solution)/shard_map/all_to_all | solution.py:69
  137.3 3.6 %copy-start.3 = (bf16[4,1,8,36,512]{4,3,2,1,0:T(8,128)(2,1)S(1)}, bf16[4,1,8,36,512]{4,3,2,1,0:T(8,128)(2,1)}, u32[]{:S(2)}) copy-start(bf16[4,1,8,36,512]{4,3,2,1,0:T(8,128)(2,1)} %get-tuple-element.19) | copy-start | bytes 3538948
  140.9 2.1 %copy-start.2 = (bf16[4,1,8,36,512]{4,3,2,1,0:T(8,128)(2,1)S(1)}, bf16[4,1,8,36,512]{4,3,2,1,0:T(8,128)(2,1)}, u32[]{:S(2)}) copy-start(bf16[4,1,8,36,512]{4,3,2,1,0:T(8,128)(2,1)} %get-tuple-element.20) | copy-start | bytes 3538948
Sparse Core Ops, SparseCore 0:
  22.7 46.6 all-gather.5
  70.9 49.7 all-gather.3
where the time goes:
time: 190 us; the launch traced here: 189 us
  blocking collectives  52.1 us (27%)
  matrix products  41.3 us (22%)
  local copies, waits for them, and re-layouts  38.8 us (20%)
  waiting for transfers between devices  37.1 us (20%)
  between operations  14.3 us (8%)
  starting transfers between devices  4.8 us (3%)
    all_gather x1, waiting for transfers between devices, per_device(): hidden_all = lax.all_gather(hidden, 'dp', axis=1, tiled=True)  37 us
    all_gather x1, blocking collectives, per_device(): lax.all_gather(gate_weights, ('expert', 'dp'), axis=0, tiled=True)  21.2 us
    dot_general x4, matrix products, per_device(): jnp.einsum('lscf,slcd->lfd', hidden_all[:, replica], scaled[:, replica],...  20.7 us
    all_gather x1, blocking collectives, per_device(): ids_all = lax.all_gather(expert_ids, ('expert', 'dp'), axis=0, tiled=True)  18.1 us
    unnamed x18, local copies, waits for them, and re-layouts  17.8 us
    all_to_all x1, blocking collectives, per_device(): cols = lax.all_to_all(cols, 'dp', split_axis=1, concat_axis=0, tiled=True)  12.9 us
    dot_general x1, matrix products, per_device(): jnp.einsum('liscf,lfd->silcd', hidden_all, down_weight, preferred_element...  11.1 us
    gather x5, local copies, waits for them, and re-layouts, per_device(): own_slot = jnp.take_along_axis(own_rank, expert_ids, axis=1)  7.34 us
  transfers between devices with their start and end apart: 3, of which 1 were waited for; matrix products, arithmetic and copies ran while one was open for 31% of the time, Pallas kernels for 0%

commit v1 on v0

--- a/solution.py
+++ b/solution.py
@@ -5,6 +5,19 @@
 
 
 def per_device(out_grad, gate_weights, expert_ids, hidden, down_weight):
+
+    def turn_unit(point):
+        piece_next = lax.axis_size(("expert", "dp"))
+        return jnp.concatenate(
+            lax.all_to_all(
+                jnp.stack([point] * piece_next),
+                axis_name=("expert", "dp"),
+                split_axis=0,
+                concat_axis=0,
+            ),
+            0,
+        )
+
     tok_rows, top_count = expert_ids.shape
     row_width = out_grad.shape[1]
     local_count = hidden.shape[0]
@@ -25,7 +38,7 @@
     grad_all = grad_all.reshape(block_count, tok_rows, col_width)
     ids_all = lax.all_gather(expert_ids, ("expert", "dp"), axis=0, tiled=True)
     ids_all = ids_all.reshape(block_count, tok_rows, top_count)
-    gate_all = lax.all_gather(gate_weights, ("expert", "dp"), axis=0, tiled=True)
+    gate_all = turn_unit(gate_weights)
     gate_all = gate_all.reshape(block_count, tok_rows, top_count)
     hidden_all = lax.all_gather(hidden, "dp", axis=1, tiled=True)
     my_experts = lax.axis_index("expert") * local_count + jnp.arange(local_count, dtype=jnp.int32)

time: 190 us -> 190 us (level)
  blocking collectives: 52.1 us -> 35.4 us
  waiting for transfers between devices: 37.1 us -> 48.2 us
  starting transfers between devices: 4.8 us -> 9.78 us
    all_gather x1 -> x0, blocking collectives: 21.2 us -> none  [per_device(): lax.all_gather(gate_weights, ('expert', 'dp'), axis=0, tiled=True)]
    all_gather x1, waiting for transfers between devices: 0.02 us -> 8.91 us  [per_device(): grad_all = lax.all_gather(cols, 'expert', axis=0, tiled=False)]
    all_to_all x0 -> x1, starting transfers between devices: none -> 4.98 us  [turn_unit(): lax.all_to_all(jnp.stack([point] * piece_next), axis_name=('expert', 'dp'...]
    all_gather x1, blocking collectives: 18.1 us -> 22.6 us  [per_device(): ids_all = lax.all_gather(expert_ids, ('expert', 'dp'), axis=0, tiled=True)]
    all_gather x1, waiting for transfers between devices: 37 us -> 39.2 us  [per_device(): hidden_all = lax.all_gather(hidden, 'dp', axis=1, tiled=True)]
  transfers between devices with their start and end apart: 3 -> 4, of which waited for: 1 -> 2; matrix products, arithmetic and copies ran while one was open for 31% -> 31% of each run, Pallas kernels for 0% -> 0%
where the time goes in v1:
time: 190 us
  waiting for transfers between devices  48.2 us (25%)
  matrix products  42.1 us (22%)
  local copies, waits for them, and re-layouts  39 us (21%)
  blocking collectives  35.4 us (19%)
  between operations  14.3 us (8%)
  starting transfers between devices  9.78 us (5%)
    all_gather x1, waiting for transfers between devices, per_device(): hidden_all = lax.all_gather(hidden, 'dp', axis=1, tiled=True)  39.2 us
    all_gather x1, blocking collectives, per_device(): ids_all = lax.all_gather(expert_ids, ('expert', 'dp'), axis=0, tiled=True)  22.6 us
    dot_general x4, matrix products, per_device(): jnp.einsum('lscf,slcd->lfd', hidden_all[:, replica], scaled[:, replica],...  20.7 us
    unnamed x18, local copies, waits for them, and re-layouts  17.3 us
    all_to_all x1, blocking collectives, per_device(): cols = lax.all_to_all(cols, 'dp', split_axis=1, concat_axis=0, tiled=True)  12.9 us
    dot_general x1, matrix products, per_device(): jnp.einsum('liscf,lfd->silcd', hidden_all, down_weight, preferred_element...  11.1 us
    all_gather x1, waiting for transfers between devices, per_device(): grad_all = lax.all_gather(cols, 'expert', axis=0, tiled=False)  8.91 us
    gather x5, local copies, waits for them, and re-layouts, per_device(): own_slot = jnp.take_along_axis(own_rank, expert_ids, axis=1)  7.34 us
  transfers between devices with their start and end apart: 4, of which 2 were waited for; matrix products, arithmetic and copies ran while one was open for 31% of the time, Pallas kernels for 0%

profile of v1, /device:TPU:0, one launch (start us, length us, event | category | flops | bytes accessed | tf_op | source)
XLA Modules:
  0.0 189.8 jit_solution(16271496279451681902)
XLA Ops:
  7.2 0.0 copy-start.1
  7.2 0.0 all-gather.6.cloned.1.call-start
  7.2 1.4 copy.113
  8.7 12.9 %all_to_all.25 = bf16[128,4,512]{0,2,1:T(8,128)(2,1)S(1)} all-to-all(bf16[128,4,512]{0,2,1:T(8,128)(2,1)S(1)} %bitcast.92), channel_id=1, replica_groups=mesh['groups'=2,'expert'=4,'dp'=4] {'dp'}, dimensions={1} | all-to-all | bytes 1048576 | tf_op jit(solution)/shard_map/all_to_all | solution.py:35
  21.5 1.0 copy.114
  22.5 0.0 all-gather.6.cloned.1.call-update
  22.6 0.0 copy-start.5
  22.6 0.0 copy-start.4
  22.6 0.0 all-gather.4.cloned.1.call-start
  22.6 0.0 copy-done.1
  22.7 1.8 copy.116
  24.4 0.0 all-gather.4.cloned.1.call-update
  24.4 0.0 copy-done.5
  24.5 0.6 stack.2
  25.1 5.0 %all-to-all-start = ((bf16[16,128,8]{1,2,0:T(8,128)(2,1)}), bf16[16,128,8]{1,2,0:T(8,128)(2,1)S(1)}, u32[]{:S(2)}, u32[]{:S(2)}) async-start(bf16[16,128,8]{1,2,0:T(8,128)(2,1)} %stack.2), calls=%async_computation | async-start | bytes 65536 | tf_op jit(solution)/shard_map/all_to_all | solution.py:12
  30.1 0.0 copy-done.4
  30.1 0.1 copy.127
  30.2 0.1 reshape.63
  30.3 0.1 convolution_convert_fusion.3
  30.4 7.0 %gather_fusion.1 = s32[1024]{0:T(1024)S(1)} fusion(s32[128,32]{0,1:T(8,128)S(1)} %convolution_convert_fusion.3, s32[1024]{0:T(1024)S(1)} %reshape.63), kind=kCustom, calls=%fused_computation.1 | custom fusion | bytes 16384 | tf_op jit(solution)/shard_map/jit(take_along_axis)/gather | solution.py:91
  37.5 0.1 reshape.66
  37.6 0.1 copy.129
  37.7 0.1 reshape.57
  37.8 22.6 %all_gather.9 = s32[2048,8]{0,1:T(8,128)S(1)} all-gather(s32[128,8]{0,1:T(8,128)S(1)} %copy-done.4), channel_id=1, replica_groups=mesh['groups'=2,'expert'=4,'dp'=4] {'expert','dp'}, dimensions={0}, use_global_device_ids=true | all-gather | bytes 69632 | tf_op jit(solution)/shard_map/all_gather | solution.py:39
  60.4 0.1 compare_reduce_fusion
  60.6 0.1 convolution_convert_fusion.2
  60.7 0.0 all-to-all-done
  60.7 0.1 fusion.21
  60.9 8.9 %all-gather.6.cloned.1.call-done = bf16[16,128,1,512]{3,1,2,0:T(8,128)(2,1)} async-done(((bf16[4,128,1,512]{3,1,2,0:T(8,128)(2,1)}), bf16[16,128,1,512]{3,1,2,0:T(8,128)(2,1)}) %all-gather.6.cloned.1.call-update) | async-done | bytes 2097168 | tf_op jit(solution)/shard_map/all_gather | solution.py:37
  69.8 3.1 %convolution_convert_fusion = bf16[16,8,36,512]{3,2,1,0:T(8,128)(2,1)S(1)} fusion(bf16[16,128,1,512]{3,1,2,0:T(8,128)(2,1)} %all-gather.6.cloned.1.call-done, bf16[16,8,128]{2,1,0:T(8,128)(2,1)S(1)} %bitcast.98, s32[16,8,128]{2,1,0:T(8,128)S(1)} %convolution_convert_fusion.2, pred[16,8,128]{2,1,0:T(8,128)(4,1)S(1)} %bitcast.95), kind=kOutput, calls=%fused_computation.12 | convolution fusion | flops 608108544 | bytes 6930432 | tf_op jit(solution)/shard_map/blct,btd->blcd/dot_general | solution.py:61
  72.9 0.0 copy-start
  72.9 2.0 %fusion.27 = (bf16[4,1,8,36,512]{4,3,2,1,0:T(8,128)(2,1)S(1)}, bf16[4,1,8,36,512]{4,3,2,1,0:T(8,128)(2,1)}, bf16[4,1,8,36,512]{4,3,2,1,0:T(8,128)(2,1)}, bf16[4,1,8,36,512]{4,3,2,1,0:T(8,128)(2,1)S(1)}) fusion(bf16[4,4,8,36,512]{4,3,2,1,0:T(8,128)(2,1)S(1)} %bitcast.90), kind=kLoop, calls=%fused_computation.54 | loop fusion | bytes 9437184 | tf_op jit(solution)/shard_map/slice | solution.py:72
  75.0 0.0 copy-done
  75.0 6.9 %bitcast_convert_fusion.4 = f32[4,4,8,36,512]{4,3,2,1,0:T(8,128)} fusion(bf16[16,128,1,512]{3,1,2,0:T(8,128)(2,1)S(1)} %copy-done, s32[16,8,128]{2,1,0:T(8,128)S(1)} %convolution_convert_fusion.2, pred[16,8,128]{2,1,0:T(8,128)(4,1)S(1)} %bitcast.96), kind=kOutput, calls=%fused_computation.51 | convolution fusion | flops 609878016 | bytes 11616256 | tf_op jit(solution)/shard_map/blct,btd->blcd/dot_general | solution.py:58
  81.9 39.2 %all-gather.4.cloned.1.call-done = bf16[8,4,4,36,768]{4,0,3,2,1:T(8,128)(2,1)} async-done(((bf16[8,1,4,36,768]{4,0,3,2,1:T(8,128)(2,1)}), bf16[8,4,4,36,768]{4,0,3,2,1:T(8,128)(2,1)}) %all-gather.4.cloned.1.call-update) | async-done | bytes 7077904 | tf_op jit(solution)/shard_map/all_gather | solution.py:43
  121.1 11.1 %fusion = f32[4,4,8,36]{3,0,1,2:T(4,128)S(1)} fusion(f32[4,4,8,36,512]{4,3,2,1,0:T(8,128)} %bitcast_convert_fusion.4, bf16[8,4,4,36,768]{4,0,3,2,1:T(8,128)(2,1)} %all-gather.4.cloned.1.call-done, bf16[8,768,512]{2,1,0:T(8,128)(2,1)} %param.9), kind=kOutput, calls=%fused_computation.8 | convolution fusion | flops 3628592640 | bytes 22824960 | tf_op jit(solution)/shard_map/liscf,lfd->silcd/dot_general | solution.py:79
  132.2 0.7 reshape.85
  132.9 4.7 %all-to-all-start.2 = ((f32[16,1,288]{2,1,0:T(1,128)}), f32[16,1,288]{2,1,0:T(1,128)S(1)}, u32[]{:S(2)}, u32[]{:S(2)}) async-start(f32[16,1,288]{2,1,0:T(1,128)} %reshape.85), calls=%async_computation.2 | async-start | bytes 49152 | tf_op jit(solution)/shard_map/all_to_all | solution.py:82
  137.7 0.0 copy-start.3
  137.7 3.6 %fusion.26 = (bf16[8,1,4,36,768]{4,0,3,2,1:T(8,128)(2,1)S(1)}, bf16[8,1,4,36,768]{4,0,3,2,1:T(8,128)(2,1)S(1)}, bf16[8,1,4,36,768]{4,0,3,2,1:T(8,128)(2,1)S(1)}, bf16[8,1,4,36,768]{4,0,3,2,1:T(8,128)(2,1)S(1)}) fusion(bf16[8,4,4,36,768]{4,0,3,2,1:T(8,128)(2,1)} %all-gather.4.cloned.1.call-done), kind=kLoop, calls=%fused_computation.53 | loop fusion | bytes 14155776 | tf_op jit(solution)/shard_map/slice | solution.py:71
  141.3 0.0 copy-done.3
  141.3 0.0 copy-start.2
  141.3 2.0 %fusion.12 = bf16[8,512,768,1]{2,1,3,0:T(8,128)(2,1)S(1)} fusion(bf16[8,1,4,36,768]{4,0,3,2,1:T(8,128)(2,1)S(1)} %get-tuple-element.15, bf16[4,1,8,36,512]{4,3,2,1,0:T(8,128)(2,1)S(1)} %copy-done.3), kind=kOutput, calls=%fused_computation.21 | convolution fusion | flops 905969664 | bytes 9240576 | tf_op jit(solution)/shard_map/lscf,slcd->lfd/dot_general | solution.py:69
  143.4 0.0 copy-done.2
  143.4 4.7 %fusion.13 = bf16[8,512,768,1]{2,1,3,0:T(8,128)(2,1)} fusion(bf16[8,1,4,36,768]{4,0,3,2,1:T(8,128)(2,1)S(1)} %get-tuple-element.16, bf16[4,1,8,36,512]{4,3,2,1,0:T(8,128)(2,1)S(1)} %copy-done.2), kind=kOutput, calls=%fused_computation.23 | convolution fusion | flops 905969664 | bytes 9240576 | tf_op jit(solution)/shard_map/lscf,slcd->lfd/dot_general | solution.py:69
  148.1 4.8 %fusion.14 = bf16[8,512,768,1]{2,1,3,0:T(8,128)(2,1)} fusion(bf16[8,1,4,36,768]{4,0,3,2,1:T(8,128)(2,1)S(1)} %get-tuple-element.17, bf16[4,1,8,36,512]{4,3,2,1,0:T(8,128)(2,1)S(1)} %get-tuple-element.21), kind=kOutput, calls=%fused_computation.25 | convolution fusion | flops 905969664 | bytes 9240576 | tf_op jit(solution)/shard_map/lscf,slcd->lfd/dot_general | solution.py:69
  152.8 9.2 %add_bitcast_fusion = f32[8,768,512]{1,2,0:T(8,128)} fusion(bf16[8,512,768,1]{2,1,3,0:T(8,128)(2,1)} %fusion.14, bf16[8,512,768,1]{2,1,3,0:T(8,128)(2,1)} %fusion.13, bf16[8,512,768,1]{2,1,3,0:T(8,128)(2,1)S(1)} %fusion.12, bf16[8,1,4,36,768]{4,0,3,2,1:T(8,128)(2,1)S(1)} %get-tuple-element.14, bf16[4,1,8,36,512]{4,3,2,1,0:T(8,128)(2,1)S(1)} %get-tuple-element.18), kind=kOutput, calls=%fused_computation.6 | convolution fusion | flops 931135488 | bytes 34406400 | tf_op jit(solution)/shard_map/lscf,slcd->lfd/dot_general | solution.py:69
  162.0 12.6 %copy.130 = f32[8,768,512]{2,1,0:T(8,128)} copy(f32[8,768,512]{1,2,0:T(8,128)} %add_bitcast_fusion) | data formatting | bytes 25165824
  174.6 0.0 all-to-all-done.2
  174.6 0.5 broadcast.39
  175.1 0.7 reduce
  175.8 0.1 reshape.86
  175.9 0.1 reshape.52
  176.1 6.2 %gather_fusion = f32[1024]{0:T(1024)S(1)} fusion(f32[1152]{0:T(1024)S(1)} %reshape.52, s32[1024]{0:T(1024)S(1)} %broadcast_clamp_fusion), kind=kCustom, calls=%fused_computation | custom fusion | bytes 12288 | tf_op jit(solution)/shard_map/gather | solution.py:92
  182.2 0.1 reshape.56
  182.3 0.7 copy.131
  (9 shorter events, 0.1 us)
Async XLA Ops:
  7.2 15.5 %copy-start.1 = (bf16[8,1,4,36,768]{4,2,3,1,0:T(4,128)(2,1)S(1)}, bf16[8,1,4,36,768]{4,2,3,1,0:T(4,128)(2,1)}, u32[]{:S(2)}) copy-start(bf16[8,1,4,36,768]{4,2,3,1,0:T(4,128)(2,1)} %param.8) | copy-start | bytes 5308420
  7.2 62.6 %all-gather.6.cloned.1.call-start = ((), (), s32[]{:S(2)}) async-start(), calls=%async_computation.4 | async-start | bytes 2621440 | tf_op jit(solution)/shard_map/all_gather | solution.py:37
  22.6 1.9 copy-start.5
  22.6 7.5 %copy-start.4 = (s32[128,8]{0,1:T(8,128)S(1)}, s32[128,8]{0,1:T(8,128)}, u32[]{:S(2)}) copy-start(s32[128,8]{0,1:T(8,128)} %param.7) | copy-start | bytes 12292
  22.6 98.5 %all-gather.4.cloned.1.call-start = ((), (), s32[]{:S(2)}) async-start(), calls=%async_computation.3 | async-start | bytes 8847360 | tf_op jit(solution)/shard_map/all_gather | solution.py:43
  25.1 35.6 %all-to-all-start = ((bf16[16,128,8]{1,2,0:T(8,128)(2,1)}), bf16[16,128,8]{1,2,0:T(8,128)(2,1)S(1)}, u32[]{:S(2)}, u32[]{:S(2)}) async-start(bf16[16,128,8]{1,2,0:T(8,128)(2,1)} %stack.2), calls=%async_computation | async-start | bytes 65536 | tf_op jit(solution)/shard_map/all_to_all | solution.py:12
  72.9 2.0 %copy-start = (bf16[16,128,1,512]{3,1,2,0:T(8,128)(2,1)S(1)}, bf16[16,128,1,512]{3,1,2,0:T(8,128)(2,1)}, u32[]{:S(2)}) copy-start(bf16[16,128,1,512]{3,1,2,0:T(8,128)(2,1)} %all-gather.6.cloned.1.call-done) | copy-start | bytes 6291460
  132.9 41.7 %all-to-all-start.2 = ((f32[16,1,288]{2,1,0:T(1,128)}), f32[16,1,288]{2,1,0:T(1,128)S(1)}, u32[]{:S(2)}, u32[]{:S(2)}) async-start(f32[16,1,288]{2,1,0:T(1,128)} %reshape.85), calls=%async_computation.2 | async-start | bytes 49152 | tf_op jit(solution)/shard_map/all_to_all | solution.py:82
  137.7 3.6 %copy-start.3 = (bf16[4,1,8,36,512]{4,3,2,1,0:T(8,128)(2,1)S(1)}, bf16[4,1,8,36,512]{4,3,2,1,0:T(8,128)(2,1)}, u32[]{:S(2)}) copy-start(bf16[4,1,8,36,512]{4,3,2,1,0:T(8,128)(2,1)} %get-tuple-element.19) | copy-start | bytes 3538948
  141.3 2.1 %copy-start.2 = (bf16[4,1,8,36,512]{4,3,2,1,0:T(8,128)(2,1)S(1)}, bf16[4,1,8,36,512]{4,3,2,1,0:T(8,128)(2,1)}, u32[]{:S(2)}) copy-start(bf16[4,1,8,36,512]{4,3,2,1,0:T(8,128)(2,1)} %get-tuple-element.20) | copy-start | bytes 3538948
Sparse Core Ops, SparseCore 0:
  22.7 47.0 all-gather.5
  71.4 49.6 all-gather.3
